TPU v7x, 32 devices: a whole 2x2x4 slice. The times are simulated.
32 devices in a mesh: groups: 2 (over x), ex: 16 (over z, y, core).
Axes of the slice: x: 2, y: 2, z: 4, core: 2. Of those that a mesh axis runs over, the one named last changes fastest.
Arguments:
- grads: bfloat16 [1024, 65536], P(('groups', 'ex')), parts along dimension 0, may hold values from -6 to 6
- proj: bfloat16 [65536, 1024], P('ex'), may hold values from -0.0234375 to 0.0234375
- target_ids: int32 [24, 128], replicated, may hold values from 0 to 511, as said below
- target_counts: int32 [24], replicated, may hold values from 1 to 128, as said below
Outputs:
- scores: float32 [1024, 24], P(('groups', 'ex')), parts along dimension 0
- sketch: float32 [1024, 1024], P(('groups', 'ex')), parts along dimension 0
There are 2 independent parts, one for each index of `groups`. A program takes and returns all parts, laid end to end along the dimension named above; an argument that names none is the same for every part. Nothing has to cross between parts.
Inputs may be any that keep to these rules, and one draw needn't show every extreme that they name: `target_ids`: indices of examples of this part; slots at or past a domain's count are ignored. `target_counts`: some domain fills all 128 slots.
All inputs are finite; a program needn't handle non-finite values.
Results may differ from a plain program's by a relative error of at most 0.0003.
Values may be sent and summed in bfloat16 or wider, within the bound.
No kernel may reach another device: no remote copies, remote signals or barrier semaphores. Data moves between devices by JAX's collectives and lax.ppermute only.
A program may use at most 128 MiB of HBM per device.

v0:
```python
import jax
import jax.numpy as jnp
from jax import lax
from jax.sharding import PartitionSpec as P


def partner(array, axis, bit):
    return lax.ppermute(array, axis, [(i, i ^ 1 << bit) for i in range(lax.axis_size(axis))])


def reduce_scatter(partial_value, bits, position):
    value = partial_value
    for level in range(bits):
        value = value.reshape((-1, 2) + value.shape[1:])
        own_bit = position // 2**level % 2
        kept = lax.dynamic_index_in_dim(value, own_bit, axis=1, keepdims=False)
        sent = lax.dynamic_index_in_dim(value, 1 - own_bit, axis=1, keepdims=False)
        value = kept + partner(sent, "ex", level)
    return value[0]


def all_gather(block, bits, position):
    value = block[None]
    for level in range(bits - 1, -1, -1):
        received = partner(value, "ex", level)
        high_side = position // 2**level % 2 == 1
        low = jnp.where(high_side, received, value)
        high = jnp.where(high_side, value, received)
        value = jnp.stack([low, high], axis=1).reshape((-1,) + value.shape[1:])
    return value


def on_device(grads, proj, target_ids, target_counts):
    count_ex = lax.axis_size("ex")
    bits = count_ex.bit_length() - 1
    position = lax.axis_index("ex")
    ex_rows = grads.shape[0]
    examples = ex_rows * count_ex
    sketch_width = proj.shape[1]
    with jax.named_scope("gradient_exchange"):
        columns = lax.all_to_all(grads, "ex", split_axis=1, concat_axis=0, tiled=True)
    with jax.named_scope("partial_projection"):
        partial_value = jnp.dot(columns, proj, preferred_element_type=jnp.float32)
    with jax.named_scope("sketch_reduce"):
        sketch = reduce_scatter(
            partial_value.reshape(count_ex, ex_rows, sketch_width), bits, position
        )
    with jax.named_scope("sketch_gather"):
        sketch_all = all_gather(sketch, bits, position).reshape(examples, sketch_width)
    slot_count = target_ids.shape[1]
    live_slot = jnp.arange(slot_count, dtype=jnp.int32)[None, :] < target_counts[:, None]
    example_index = jnp.arange(examples, dtype=jnp.int32)
    matches = (target_ids[:, :, None] == example_index[None, None, :]) & live_slot[:, :, None]
    weight = jnp.sum(matches.astype(jnp.float32), axis=1) / target_counts[:, None].astype(
        jnp.float32
    )
    if examples < sketch_width:
        with jax.named_scope("kernel_matrix"):
            kernel = jnp.dot(sketch_all, sketch_all.T, precision=lax.Precision.HIGHEST)
        with jax.named_scope("kernel_solve"):
            system = kernel / jnp.float32(examples) + 0.1 * jnp.eye(examples, dtype=jnp.float32)
            factor = jnp.linalg.cholesky(system)
            middle = lax.linalg.triangular_solve(factor, weight.T, left_side=True, lower=True)
            coeffs = lax.linalg.triangular_solve(
                factor, middle, left_side=True, lower=True, transpose_a=True
            )
        own_kernel = lax.dynamic_slice_in_dim(kernel, position * ex_rows, ex_rows, axis=0)
        scores = jnp.dot(own_kernel, coeffs, precision=lax.Precision.HIGHEST)
    else:
        with jax.named_scope("gram_solve"):
            gram_matrix = jnp.dot(sketch_all.T, sketch_all, precision=lax.Precision.HIGHEST)
            domain = jnp.dot(weight, sketch_all, precision=lax.Precision.HIGHEST)
            hessian = gram_matrix / jnp.float32(examples) + 0.1 * jnp.eye(
                sketch_width, dtype=jnp.float32
            )
            factor = jnp.linalg.cholesky(hessian)
            middle = lax.linalg.triangular_solve(factor, domain.T, left_side=True, lower=True)
            solved = lax.linalg.triangular_solve(
                factor, middle, left_side=True, lower=True, transpose_a=True
            )
        scores = jnp.dot(sketch, solved, precision=lax.Precision.HIGHEST)
    return (scores, sketch)


def solution(mesh):
    placed = (P(("groups", "ex"), None), P("ex", None), P(), P())
    return jax.shard_map(
        on_device,
        mesh=mesh,
        in_specs=placed,
        out_specs=(P(("groups", "ex"), None), P(("groups", "ex"), None)),
        check_vma=False,
    )
```

profile of v0, /device:TPU:0, one launch (start us, length us, event | category | flops | bytes accessed | tf_op | source)
XLA Modules:
  0.0 324.4 jit_solution(8416492365125750362)
XLA Ops:
  0.6 4.7 %copy.26 = bf16[4,16,8,4096]{3,2,0,1:T(8,128)(2,1)} copy(bf16[4,16,8,4096]{3,2,1,0:T(8,128)(2,1)} %bitcast.121) | data formatting | bytes 8388608 | tf_op jit(solution)/shard_map/gradient_exchange/all_to_all | solution.py:41
  5.3 7.4 %all-to-all-start = ((bf16[32,16,4096]{2,0,1:T(8,128)(2,1)}), bf16[32,16,4096]{2,0,1:T(8,128)(2,1)}, u32[]{:S(2)}, u32[]{:S(2)}) async-start(bf16[32,16,4096]{2,0,1:T(8,128)(2,1)} %bitcast.119), calls=%async_computation | async-start | bytes 8388608 | tf_op jit(solution)/shard_map/gradient_exchange/all_to_all | solution.py:41
  12.7 77.7 %all-to-all-done = bf16[32,16,4096]{2,0,1:T(8,128)(2,1)} async-done(((bf16[32,16,4096]{2,0,1:T(8,128)(2,1)}), bf16[32,16,4096]{2,0,1:T(8,128)(2,1)}, u32[]{:S(2)}, u32[]{:S(2)}) %all-to-all-start) | async-done | bytes 4194336 | tf_op jit(solution)/shard_map/gradient_exchange/all_to_all | solution.py:41
  90.4 8.1 %fusion = f32[8,2,32,1024]{3,2,1,0:T(8,128)S(1)} fusion(bf16[8,2,32,4096]{3,2,1,0:T(8,128)(2,1)} %bitcast.1, bf16[4096,1024]{1,0:T(8,128)(2,1)} %param.5), kind=kOutput, calls=%fused_computation.2 | convolution fusion | flops 4294967296 | bytes 14680064 | tf_op jit(solution)/shard_map/partial_projection/dot_general | solution.py:43
  98.7 0.8 collective-permute-start
  99.5 2.4 collective-permute-done
  101.9 1.4 bitcast_add_fusion
  103.3 6.3 %collective-permute-start.1 = (f32[4,32,1024]{2,1,0:T(8,128)S(1)}, f32[4,32,1024]{2,1,0:T(8,128)S(1)}, u32[]{:S(2)}, u32[]{:S(2)}) collective-permute-start(f32[4,32,1024]{2,1,0:T(8,128)S(1)} %dynamic-slice_bitcast_fusion.1), channel_id=1, source_target_pairs={{0,2},{1,3},{2,0},{3,1},{4,6},{5,7},{6,4},{7,5},{8,10},{9,11},{10,... | collective-permute-start | bytes 1572872 | tf_op jit(solution)/shard_map/sketch_reduce/ppermute | solution.py:8
  109.6 12.4 %collective-permute-done.1 = f32[4,32,1024]{2,1,0:T(8,128)S(1)} collective-permute-done((f32[4,32,1024]{2,1,0:T(8,128)S(1)}, f32[4,32,1024]{2,1,0:T(8,128)S(1)}, u32[]{:S(2)}, u32[]{:S(2)}) %collective-permute-start.1) | collective-permute-done | bytes 524320 | tf_op jit(solution)/shard_map/sketch_reduce/ppermute | solution.py:8
  122.2 11.4 %collective-permute-start.2 = (f32[2,32,1024]{2,1,0:T(8,128)S(1)}, f32[2,32,1024]{2,1,0:T(8,128)S(1)}, u32[]{:S(2)}, u32[]{:S(2)}) collective-permute-start(f32[2,32,1024]{2,1,0:T(8,128)S(1)} %dynamic-slice_bitcast_fusion.2), channel_id=1, source_target_pairs={{0,4},{1,5},{2,6},{3,7},{4,0},{5,1},{6,2},{7,3},{8,12},{9,13},{10,... | collective-permute-start | bytes 786440 | tf_op jit(solution)/shard_map/sketch_reduce/ppermute | solution.py:8
  133.6 6.3 %collective-permute-done.2 = f32[2,32,1024]{2,1,0:T(8,128)S(1)} collective-permute-done((f32[2,32,1024]{2,1,0:T(8,128)S(1)}, f32[2,32,1024]{2,1,0:T(8,128)S(1)}, u32[]{:S(2)}, u32[]{:S(2)}) %collective-permute-start.2) | collective-permute-done | bytes 262176 | tf_op jit(solution)/shard_map/sketch_reduce/ppermute | solution.py:8
  139.9 2.7 collective-permute-start.3
  142.6 5.7 %collective-permute-done.3 = f32[1,32,1024]{2,1,0:T(8,128)S(1)} collective-permute-done((f32[1,32,1024]{2,1,0:T(8,128)S(1)}, f32[1,32,1024]{2,1,0:T(8,128)S(1)}, u32[]{:S(2)}, u32[]{:S(2)}) %collective-permute-start.3) | collective-permute-done | bytes 131104 | tf_op jit(solution)/shard_map/sketch_reduce/ppermute | solution.py:8
  148.4 0.3 collective-permute-start.4
  148.7 7.9 %collective-permute-done.4 = f32[1,32,1024]{2,1,0:T(8,128)S(1)} collective-permute-done((f32[1,32,1024]{2,1,0:T(8,128)S(1)}, f32[1,32,1024]{2,1,0:T(8,128)S(1)}, u32[]{:S(2)}, u32[]{:S(2)}) %collective-permute-start.4) | collective-permute-done | bytes 131104 | tf_op jit(solution)/shard_map/sketch_gather/ppermute | solution.py:8
  156.7 8.2 %collective-permute-done.5 = f32[2,32,1024]{2,1,0:T(8,128)S(1)} collective-permute-done((f32[2,32,1024]{2,1,0:T(8,128)S(1)}, f32[2,32,1024]{2,1,0:T(8,128)S(1)}, u32[]{:S(2)}, u32[]{:S(2)}) %collective-permute-start.5) | collective-permute-done | bytes 262176 | tf_op jit(solution)/shard_map/sketch_gather/ppermute | solution.py:8
  165.1 13.0 %collective-permute-done.6 = f32[4,32,1024]{2,1,0:T(8,128)S(1)} collective-permute-done((f32[4,32,1024]{2,1,0:T(8,128)S(1)}, f32[4,32,1024]{2,1,0:T(8,128)S(1)}, u32[]{:S(2)}, u32[]{:S(2)}) %collective-permute-start.6) | collective-permute-done | bytes 524320 | tf_op jit(solution)/shard_map/sketch_gather/ppermute | solution.py:8
  178.5 0.4 copy-done.2
  178.9 2.0 convert_reduce_fusion
  181.1 0.2 select_bitcast_fusion.1
  181.4 0.2 pad_maximum_fusion
  181.6 0.2 copy.21
  181.9 3.5 %fusion.61 = f32[512,512]{1,0:T(8,128)S(1)} fusion(f32[512,1024]{1,0:T(8,128)S(1)} %bitcast.118), kind=kOutput, calls=%fused_computation.127 | convolution fusion | flops 3221225472 | bytes 3145728 | tf_op jit(solution)/shard_map/kernel_matrix/dot_general | solution.py:59
  185.5 0.3 copy.22
  185.9 0.2 add_multiply_fusion
  186.1 11.7 %cholesky.103 = f32[128,128]{1,0:T(8,128)S(1)} custom-call(f32[128,128]{1,0:T(8,128)S(1)} %cholesky.263), custom_call_target="Cholesky" | custom-call | tf_op jit(solution)/shard_map/kernel_solve/jit(cholesky)/cholesky | solution.py:62
  198.0 9.8 %custom-call.32 = f32[1,128,128]{1,2,0:T(8,128)S(1)} custom-call(f32[1,128,128]{2,1,0:T(8,128)S(1)} %get-tuple-element.37), custom_call_target="InvertDiagBlocksLowerTriangular" | custom-call | tf_op jit(solution)/shard_map/kernel_solve/jit(cholesky)/cholesky | solution.py:62
  207.8 0.3 constant_dynamic-update-slice_fusion
  208.1 0.3 convolution_subtract_fusion
  208.5 11.9 %cholesky.215 = f32[128,128]{1,0:T(8,128)S(1)} custom-call(f32[128,128]{1,0:T(8,128)S(1)} %cholesky.267), custom_call_target="Cholesky" | custom-call | tf_op jit(solution)/shard_map/kernel_solve/jit(cholesky)/cholesky | solution.py:62
  220.4 9.8 %custom-call.33 = f32[1,128,128]{1,2,0:T(8,128)S(1)} custom-call(f32[1,128,128]{2,1,0:T(8,128)S(1)} %get-tuple-element.34), custom_call_target="InvertDiagBlocksLowerTriangular" | custom-call | tf_op jit(solution)/shard_map/kernel_solve/jit(cholesky)/cholesky | solution.py:62
  230.2 0.3 convolution_dynamic-update-slice_fusion
  230.5 0.4 convolution_subtract_fusion.1
  230.9 11.7 %cholesky.236 = f32[128,128]{1,0:T(8,128)S(1)} custom-call(f32[128,128]{1,0:T(8,128)S(1)} %cholesky.272), custom_call_target="Cholesky" | custom-call | tf_op jit(solution)/shard_map/kernel_solve/jit(cholesky)/cholesky | solution.py:62
  242.6 9.8 %custom-call.34 = f32[1,128,128]{1,2,0:T(8,128)S(1)} custom-call(f32[1,128,128]{2,1,0:T(8,128)S(1)} %get-tuple-element.31), custom_call_target="InvertDiagBlocksLowerTriangular" | custom-call | tf_op jit(solution)/shard_map/kernel_solve/jit(cholesky)/cholesky | solution.py:62
  252.5 0.2 convolution_dynamic-update-slice_fusion.1
  252.7 0.6 convolution_subtract_fusion.2
  253.3 11.7 %cholesky.253 = f32[128,128]{1,0:T(8,128)S(1)} custom-call(f32[128,128]{1,0:T(8,128)S(1)} %convolution_subtract_fusion.2), custom_call_target="Cholesky" | custom-call | tf_op jit(solution)/shard_map/kernel_solve/jit(cholesky)/cholesky | solution.py:62
  265.0 0.7 compare_reduce_fusion.1
  265.7 0.7 compare_reduce_fusion
  266.4 0.7 compare_reduce_fusion.2
  269.7 10.5 %while.1 = (s32[]{:T(128)}, f32[512,512]{1,0:T(8,128)S(1)}, s32[4,2]{0,1:T(2,128)S(1)}, f32[4,128,128]{2,1,0:T(8,128)}, s32[]{:T(128)}) while((s32[]{:T(128)}, f32[512,512]{1,0:T(8,128)S(1)}, s32[4,2]{0,1:T(2,128)S(1)}, f32[4,128,128]{2,1,0:T(8,128)}, s32[]{:T(128)}) %tuple.35), condition=%wide.while_cond, body=%wide.while_body.sunk | while | flops 2 | bytes 132205 | solution.py:64
  269.8 0.6 fusion.76
  270.4 2.0 bitcast_dynamic-update-slice_fusion.2
  272.4 0.6 fusion.76
  273.0 2.0 bitcast_dynamic-update-slice_fusion.2
  275.1 0.6 fusion.76
  275.6 2.0 bitcast_dynamic-update-slice_fusion.2
  277.7 0.6 fusion.76
  278.3 2.0 bitcast_dynamic-update-slice_fusion.2
  280.2 40.1 %custom-call.35 = f32[4,128,128]{1,2,0:T(8,128)S(1)} custom-call(f32[4,128,128]{2,1,0:T(8,128)} %get-tuple-element.9), custom_call_target="InvertDiagBlocksLowerTriangular" | custom-call | tf_op jit(solution)/shard_map/kernel_solve/triangular_solve | solution.py:64
  320.5 0.2 convolution_subtract_fusion.8
  320.7 0.2 fusion.25
  320.9 0.2 convolution_subtract_fusion.7
  321.3 0.3 convolution_subtract_fusion.6
  321.6 0.2 fusion.29
  321.8 0.2 fusion.28
  322.1 0.2 convolution_subtract_fusion.5
  322.3 0.2 fusion.26
  322.5 0.2 convolution_subtract_fusion.4
  322.7 0.2 fusion.24
  322.9 0.3 convolution_subtract_fusion.3
  323.2 0.2 fusion.22
  323.4 0.8 fusion.20
  (45 shorter events, 2.4 us)
Async XLA Ops:
  5.3 85.1 %all-to-all-start = ((bf16[32,16,4096]{2,0,1:T(8,128)(2,1)}), bf16[32,16,4096]{2,0,1:T(8,128)(2,1)}, u32[]{:S(2)}, u32[]{:S(2)}) async-start(bf16[32,16,4096]{2,0,1:T(8,128)(2,1)} %bitcast.119), calls=%async_computation | async-start | bytes 8388608 | tf_op jit(solution)/shard_map/gradient_exchange/all_to_all | solution.py:41
  98.7 3.3 %collective-permute-start = (f32[8,32,1024]{2,1,0:T(8,128)S(1)}, f32[8,32,1024]{2,1,0:T(8,128)}, u32[]{:S(2)}, u32[]{:S(2)}) collective-permute-start(f32[8,32,1024]{2,1,0:T(8,128)S(1)} %dynamic-slice_bitcast_fusion), channel_id=1, source_target_pairs={{0,1},{1,0},{2,3},{3,2},{4,5},{5,4},{6,7},{7,6},{8,9},{9,8},{10,11... | collective-permute-start | bytes 3145736 | tf_op jit(solution)/shard_map/sketch_reduce/ppermute | solution.py:8
  103.3 18.7 %collective-permute-start.1 = (f32[4,32,1024]{2,1,0:T(8,128)S(1)}, f32[4,32,1024]{2,1,0:T(8,128)S(1)}, u32[]{:S(2)}, u32[]{:S(2)}) collective-permute-start(f32[4,32,1024]{2,1,0:T(8,128)S(1)} %dynamic-slice_bitcast_fusion.1), channel_id=1, source_target_pairs={{0,2},{1,3},{2,0},{3,1},{4,6},{5,7},{6,4},{7,5},{8,10},{9,11},{10,... | collective-permute-start | bytes 1572872 | tf_op jit(solution)/shard_map/sketch_reduce/ppermute | solution.py:8
  122.2 17.7 %collective-permute-start.2 = (f32[2,32,1024]{2,1,0:T(8,128)S(1)}, f32[2,32,1024]{2,1,0:T(8,128)S(1)}, u32[]{:S(2)}, u32[]{:S(2)}) collective-permute-start(f32[2,32,1024]{2,1,0:T(8,128)S(1)} %dynamic-slice_bitcast_fusion.2), channel_id=1, source_target_pairs={{0,4},{1,5},{2,6},{3,7},{4,0},{5,1},{6,2},{7,3},{8,12},{9,13},{10,... | collective-permute-start | bytes 786440 | tf_op jit(solution)/shard_map/sketch_reduce/ppermute | solution.py:8
  139.9 8.4 %collective-permute-start.3 = (f32[1,32,1024]{2,1,0:T(8,128)S(1)}, f32[1,32,1024]{2,1,0:T(8,128)S(1)}, u32[]{:S(2)}, u32[]{:S(2)}) collective-permute-start(f32[1,32,1024]{2,1,0:T(8,128)S(1)} %constant_dynamic-slice_fusion.1), channel_id=1, source_target_pairs={{0,8},{1,9},{2,10},{3,11},{4,12},{5,13},{6,14},{7,15},{8,0},{9,1},... | collective-permute-start | bytes 393224 | tf_op jit(solution)/shard_map/sketch_reduce/ppermute | solution.py:8
  148.3 29.9 %copy-start = (f32[1,32,1024]{2,1,0:T(8,128)}, f32[1,32,1024]{2,1,0:T(8,128)S(1)}, u32[]{:S(2)}) copy-start(f32[1,32,1024]{2,1,0:T(8,128)S(1)} %dynamic-slice_add_fusion) | copy-start | bytes 393220
  148.4 8.2 %collective-permute-start.4 = (f32[1,32,1024]{2,1,0:T(8,128)S(1)}, f32[1,32,1024]{2,1,0:T(8,128)S(1)}, u32[]{:S(2)}, u32[]{:S(2)}) collective-permute-start(f32[1,32,1024]{2,1,0:T(8,128)S(1)} %dynamic-slice_add_fusion), channel_id=1, source_target_pairs={{0,8},{1,9},{2,10},{3,11},{4,12},{5,13},{6,14},{7,15},{8,0},{9,1},... | collective-permute-start | bytes 393224 | tf_op jit(solution)/shard_map/sketch_gather/ppermute | solution.py:8
  156.6 8.3 %collective-permute-start.5 = (f32[2,32,1024]{2,1,0:T(8,128)S(1)}, f32[2,32,1024]{2,1,0:T(8,128)S(1)}, u32[]{:S(2)}, u32[]{:S(2)}) collective-permute-start(f32[2,32,1024]{2,1,0:T(8,128)S(1)} %maximum_bitcast_fusion), channel_id=1, source_target_pairs={{0,4},{1,5},{2,6},{3,7},{4,0},{5,1},{6,2},{7,3},{8,12},{9,13},{10,... | collective-permute-start | bytes 786440 | tf_op jit(solution)/shard_map/sketch_gather/ppermute | solution.py:8
  165.0 13.1 %collective-permute-start.6 = (f32[4,32,1024]{2,1,0:T(8,128)S(1)}, f32[4,32,1024]{2,1,0:T(8,128)S(1)}, u32[]{:S(2)}, u32[]{:S(2)}) collective-permute-start(f32[4,32,1024]{2,1,0:T(8,128)S(1)} %bitcast.124), channel_id=1, source_target_pairs={{0,2},{1,3},{2,0},{3,1},{4,6},{5,7},{6,4},{7,5},{8,10},{9,11},{10,... | collective-permute-start | bytes 1572872 | tf_op jit(solution)/shard_map/sketch_gather/ppermute | solution.py:8
  178.2 0.7 copy-start.2
  178.2 0.7 copy-start.1
  178.4 2.7 collective-permute-start.7
where the time goes:
time: 328 us; the launch traced here: 324 us
  waiting for transfers between devices  134 us (41%)
  other arithmetic  124 us (38%)
  starting transfers between devices  29.1 us (9%)
  matrix products  17.5 us (5%)
  local copies, waits for them, and re-layouts  16.5 us (5%)
  between operations  3.86 us (1%)
    another operation x14, other arithmetic, on_device(): factor = jnp.linalg.cholesky(system)  78.7 us
    all_to_all x1, waiting for transfers between devices, on_device(): lax.all_to_all(grads, 'ex', split_axis=1, concat_axis=0, tiled=True)  77.7 us
    ppermute x8, waiting for transfers between devices, partner(): lax.ppermute(array, axis, [(i, i ^ 1 << bit) for i in range(lax.axis_size...  56.1 us
    another operation x3, other arithmetic, on_device(): lax.linalg.triangular_solve(factor, middle, left_side=True, lower=True, t...  40.2 us
    ppermute x8, starting transfers between devices, partner(): lax.ppermute(array, axis, [(i, i ^ 1 << bit) for i in range(lax.axis_size...  21.7 us
    another operation x12, local copies, waits for them, and re-layouts  10.5 us
    dot_general x1, matrix products, on_device(): partial_value = jnp.dot(columns, proj, preferred_element_type=jnp.float32)  8.14 us
    all_to_all x1, starting transfers between devices, on_device(): lax.all_to_all(grads, 'ex', split_axis=1, concat_axis=0, tiled=True)  7.44 us
  transfers between devices with their start and end apart: 9, of which 9 were waited for; matrix products, arithmetic and copies ran while one was open for 1% of the time, Pallas kernels for 0%

commit v1 on v0

--- a/solution.py
+++ b/solution.py
@@ -38,7 +38,17 @@
     examples = ex_rows * count_ex
     sketch_width = proj.shape[1]
     with jax.named_scope("gradient_exchange"):
-        columns = lax.all_to_all(grads, "ex", split_axis=1, concat_axis=0, tiled=True)
+
+        def _answer_heaps(vals, where_dim, dim_no=0):
+            v1 = jnp.concatenate(
+                lax.all_to_all(
+                    jnp.stack(jnp.split(vals, lax.axis_size("ex"), axis=where_dim)), "ex", 0, 0
+                ),
+                axis=dim_no,
+            )
+            return v1
+
+        columns = _answer_heaps(grads, 1)
     with jax.named_scope("partial_projection"):
         partial_value = jnp.dot(columns, proj, preferred_element_type=jnp.float32)
     with jax.named_scope("sketch_reduce"):

time: 328 us -> 351 us (1.070)
  local copies, waits for them, and re-layouts: 16.5 us -> 38.3 us
    unnamed x6 -> x21, local copies, waits for them, and re-layouts: 0.37 us -> 25.1 us
    all_to_all x1 -> x0, local copies, waits for them, and re-layouts: 4.66 us -> none  [on_device(): lax.all_to_all(grads, 'ex', split_axis=1, concat_axis=0, tiled=True)]
    another operation x12 -> x13, local copies, waits for them, and re-layouts: 10.5 us -> 12.2 us
where the time goes in v1:
time: 351 us; the launch traced here: 347 us
  waiting for transfers between devices  134 us (38%)
  other arithmetic  124 us (35%)
  local copies, waits for them, and re-layouts  38.3 us (11%)
  starting transfers between devices  29.1 us (8%)
  matrix products  17.5 us (5%)
  between operations  3.89 us (1%)
    another operation x14, other arithmetic, on_device(): factor = jnp.linalg.cholesky(system)  78.7 us
    all_to_all x1, waiting for transfers between devices, _answer_heaps(): lax.all_to_all(jnp.stack(jnp.split(vals, lax.axis_size('ex'), axis=where_...  77.7 us
    ppermute x8, waiting for transfers between devices, partner(): lax.ppermute(array, axis, [(i, i ^ 1 << bit) for i in range(lax.axis_size...  56.4 us
    another operation x3, other arithmetic, on_device(): lax.linalg.triangular_solve(factor, middle, left_side=True, lower=True, t...  40.3 us
    unnamed x21, local copies, waits for them, and re-layouts  25.1 us
    ppermute x8, starting transfers between devices, partner(): lax.ppermute(array, axis, [(i, i ^ 1 << bit) for i in range(lax.axis_size...  21.7 us
    another operation x12, local copies, waits for them, and re-layouts  10.5 us
    dot_general x1, matrix products, on_device(): partial_value = jnp.dot(columns, proj, preferred_element_type=jnp.float32)  8.14 us
  transfers between devices with their start and end apart: 9, of which 9 were waited for; matrix products, arithmetic and copies ran while one was open for 1% of the time, Pallas kernels for 0%

profile of v1, /device:TPU:0, one launch (start us, length us, event | category | flops | bytes accessed | tf_op | source)
XLA Modules:
  0.0 346.5 jit_solution(18422283665668879057)
XLA Ops:
  0.6 1.7 bitcast_dynamic-update-slice_fusion.16
  2.3 1.7 bitcast_dynamic-update-slice_fusion.15
  4.0 1.7 bitcast_dynamic-update-slice_fusion.14
  5.6 1.7 bitcast_dynamic-update-slice_fusion.13
  7.3 1.7 bitcast_dynamic-update-slice_fusion.12
  9.0 1.7 bitcast_dynamic-update-slice_fusion.11
  10.7 1.7 bitcast_dynamic-update-slice_fusion.10
  12.3 1.7 bitcast_dynamic-update-slice_fusion.9
  14.0 1.7 bitcast_dynamic-update-slice_fusion.8
  15.7 1.7 bitcast_dynamic-update-slice_fusion.7
  17.4 1.7 bitcast_dynamic-update-slice_fusion.6
  19.1 1.7 bitcast_dynamic-update-slice_fusion.5
  20.7 1.7 bitcast_dynamic-update-slice_fusion.4
  22.4 1.7 bitcast_dynamic-update-slice_fusion.3
  24.1 1.7 bitcast_dynamic-update-slice_fusion.2
  25.7 1.7 bitcast_dynamic-update-slice_fusion.1
  27.4 7.4 %all-to-all-start = ((bf16[16,32,4096]{2,1,0:T(8,128)(2,1)}), bf16[16,32,4096]{2,1,0:T(8,128)(2,1)}, u32[]{:S(2)}, u32[]{:S(2)}) async-start(bf16[16,32,4096]{2,1,0:T(8,128)(2,1)} %bitcast_dynamic-update-slice_fusion.1), calls=%async_computation | async-start | bytes 8388608 | tf_op jit(solution)/shard_map/gradient_exchange/all_to_all | solution.py:44
  34.9 77.7 %all-to-all-done = bf16[16,32,4096]{2,1,0:T(8,128)(2,1)} async-done(((bf16[16,32,4096]{2,1,0:T(8,128)(2,1)}), bf16[16,32,4096]{2,1,0:T(8,128)(2,1)}, u32[]{:S(2)}, u32[]{:S(2)}) %all-to-all-start) | async-done | bytes 4194336 | tf_op jit(solution)/shard_map/gradient_exchange/all_to_all | solution.py:44
  112.5 8.1 %fusion = f32[8,2,32,1024]{3,2,1,0:T(8,128)S(1)} fusion(bf16[8,2,32,4096]{3,2,1,0:T(8,128)(2,1)} %bitcast.16, bf16[4096,1024]{1,0:T(8,128)(2,1)} %param.5), kind=kOutput, calls=%fused_computation.2 | convolution fusion | flops 4294967296 | bytes 14680064 | tf_op jit(solution)/shard_map/partial_projection/dot_general | solution.py:53
  120.8 0.8 collective-permute-start
  121.6 2.4 collective-permute-done
  124.0 1.4 bitcast_add_fusion
  125.5 6.3 %collective-permute-start.1 = (f32[4,32,1024]{2,1,0:T(8,128)S(1)}, f32[4,32,1024]{2,1,0:T(8,128)S(1)}, u32[]{:S(2)}, u32[]{:S(2)}) collective-permute-start(f32[4,32,1024]{2,1,0:T(8,128)S(1)} %dynamic-slice_bitcast_fusion.1), channel_id=1, source_target_pairs={{0,2},{1,3},{2,0},{3,1},{4,6},{5,7},{6,4},{7,5},{8,10},{9,11},{10,... | collective-permute-start | bytes 1572872 | tf_op jit(solution)/shard_map/sketch_reduce/ppermute | solution.py:8
  131.7 12.4 %collective-permute-done.1 = f32[4,32,1024]{2,1,0:T(8,128)S(1)} collective-permute-done((f32[4,32,1024]{2,1,0:T(8,128)S(1)}, f32[4,32,1024]{2,1,0:T(8,128)S(1)}, u32[]{:S(2)}, u32[]{:S(2)}) %collective-permute-start.1) | collective-permute-done | bytes 524320 | tf_op jit(solution)/shard_map/sketch_reduce/ppermute | solution.py:8
  144.3 11.4 %collective-permute-start.2 = (f32[2,32,1024]{2,1,0:T(8,128)S(1)}, f32[2,32,1024]{2,1,0:T(8,128)S(1)}, u32[]{:S(2)}, u32[]{:S(2)}) collective-permute-start(f32[2,32,1024]{2,1,0:T(8,128)S(1)} %dynamic-slice_bitcast_fusion.2), channel_id=1, source_target_pairs={{0,4},{1,5},{2,6},{3,7},{4,0},{5,1},{6,2},{7,3},{8,12},{9,13},{10,... | collective-permute-start | bytes 786440 | tf_op jit(solution)/shard_map/sketch_reduce/ppermute | solution.py:8
  155.7 6.3 %collective-permute-done.2 = f32[2,32,1024]{2,1,0:T(8,128)S(1)} collective-permute-done((f32[2,32,1024]{2,1,0:T(8,128)S(1)}, f32[2,32,1024]{2,1,0:T(8,128)S(1)}, u32[]{:S(2)}, u32[]{:S(2)}) %collective-permute-start.2) | collective-permute-done | bytes 262176 | tf_op jit(solution)/shard_map/sketch_reduce/ppermute | solution.py:8
  162.0 2.7 collective-permute-start.3
  164.7 5.7 %collective-permute-done.3 = f32[1,32,1024]{2,1,0:T(8,128)S(1)} collective-permute-done((f32[1,32,1024]{2,1,0:T(8,128)S(1)}, f32[1,32,1024]{2,1,0:T(8,128)S(1)}, u32[]{:S(2)}, u32[]{:S(2)}) %collective-permute-start.3) | collective-permute-done | bytes 131104 | tf_op jit(solution)/shard_map/sketch_reduce/ppermute | solution.py:8
  170.5 0.3 collective-permute-start.4
  170.8 7.9 %collective-permute-done.4 = f32[1,32,1024]{2,1,0:T(8,128)S(1)} collective-permute-done((f32[1,32,1024]{2,1,0:T(8,128)S(1)}, f32[1,32,1024]{2,1,0:T(8,128)S(1)}, u32[]{:S(2)}, u32[]{:S(2)}) %collective-permute-start.4) | collective-permute-done | bytes 131104 | tf_op jit(solution)/shard_map/sketch_gather/ppermute | solution.py:8
  178.8 8.2 %collective-permute-done.5 = f32[2,32,1024]{2,1,0:T(8,128)S(1)} collective-permute-done((f32[2,32,1024]{2,1,0:T(8,128)S(1)}, f32[2,32,1024]{2,1,0:T(8,128)S(1)}, u32[]{:S(2)}, u32[]{:S(2)}) %collective-permute-start.5) | collective-permute-done | bytes 262176 | tf_op jit(solution)/shard_map/sketch_gather/ppermute | solution.py:8
  187.2 13.0 %collective-permute-done.6 = f32[4,32,1024]{2,1,0:T(8,128)S(1)} collective-permute-done((f32[4,32,1024]{2,1,0:T(8,128)S(1)}, f32[4,32,1024]{2,1,0:T(8,128)S(1)}, u32[]{:S(2)}, u32[]{:S(2)}) %collective-permute-start.6) | collective-permute-done | bytes 524320 | tf_op jit(solution)/shard_map/sketch_gather/ppermute | solution.py:8
  200.7 2.0 convert_reduce_fusion
  202.8 0.4 collective-permute-done.7
  204.0 3.5 %fusion.61 = f32[512,512]{1,0:T(8,128)S(1)} fusion(f32[512,1024]{1,0:T(8,128)S(1)} %bitcast.144), kind=kOutput, calls=%fused_computation.142 | convolution fusion | flops 3221225472 | bytes 3145728 | tf_op jit(solution)/shard_map/kernel_matrix/dot_general | solution.py:69
  207.6 0.3 copy.18
  208.2 11.7 %cholesky.103 = f32[128,128]{1,0:T(8,128)S(1)} custom-call(f32[128,128]{1,0:T(8,128)S(1)} %cholesky.263), custom_call_target="Cholesky" | custom-call | tf_op jit(solution)/shard_map/kernel_solve/jit(cholesky)/cholesky | solution.py:72
  220.1 9.8 %custom-call.32 = f32[1,128,128]{1,2,0:T(8,128)S(1)} custom-call(f32[1,128,128]{2,1,0:T(8,128)S(1)} %get-tuple-element.37), custom_call_target="InvertDiagBlocksLowerTriangular" | custom-call | tf_op jit(solution)/shard_map/kernel_solve/jit(cholesky)/cholesky | solution.py:72
  229.9 0.3 constant_dynamic-update-slice_fusion
  230.2 0.3 convolution_subtract_fusion
  230.6 11.9 %cholesky.215 = f32[128,128]{1,0:T(8,128)S(1)} custom-call(f32[128,128]{1,0:T(8,128)S(1)} %cholesky.267), custom_call_target="Cholesky" | custom-call | tf_op jit(solution)/shard_map/kernel_solve/jit(cholesky)/cholesky | solution.py:72
  242.5 9.8 %custom-call.33 = f32[1,128,128]{1,2,0:T(8,128)S(1)} custom-call(f32[1,128,128]{2,1,0:T(8,128)S(1)} %get-tuple-element.34), custom_call_target="InvertDiagBlocksLowerTriangular" | custom-call | tf_op jit(solution)/shard_map/kernel_solve/jit(cholesky)/cholesky | solution.py:72
  252.3 0.3 convolution_dynamic-update-slice_fusion
  252.6 0.4 convolution_subtract_fusion.1
  253.0 11.7 %cholesky.236 = f32[128,128]{1,0:T(8,128)S(1)} custom-call(f32[128,128]{1,0:T(8,128)S(1)} %cholesky.272), custom_call_target="Cholesky" | custom-call | tf_op jit(solution)/shard_map/kernel_solve/jit(cholesky)/cholesky | solution.py:72
  264.7 9.8 %custom-call.34 = f32[1,128,128]{1,2,0:T(8,128)S(1)} custom-call(f32[1,128,128]{2,1,0:T(8,128)S(1)} %get-tuple-element.31), custom_call_target="InvertDiagBlocksLowerTriangular" | custom-call | tf_op jit(solution)/shard_map/kernel_solve/jit(cholesky)/cholesky | solution.py:72
  274.8 0.6 convolution_subtract_fusion.2
  275.4 11.7 %cholesky.253 = f32[128,128]{1,0:T(8,128)S(1)} custom-call(f32[128,128]{1,0:T(8,128)S(1)} %convolution_subtract_fusion.2), custom_call_target="Cholesky" | custom-call | tf_op jit(solution)/shard_map/kernel_solve/jit(cholesky)/cholesky | solution.py:72
  287.1 0.7 compare_reduce_fusion.1
  287.8 0.7 compare_reduce_fusion
  288.5 0.7 compare_reduce_fusion.2
  291.8 10.5 %while.1 = (s32[]{:T(128)}, f32[512,512]{1,0:T(8,128)S(1)}, s32[4,2]{0,1:T(2,128)S(1)}, f32[4,128,128]{2,1,0:T(8,128)}, s32[]{:T(128)}) while((s32[]{:T(128)}, f32[512,512]{1,0:T(8,128)S(1)}, s32[4,2]{0,1:T(2,128)S(1)}, f32[4,128,128]{2,1,0:T(8,128)}, s32[]{:T(128)}) %tuple.35), condition=%wide.while_cond, body=%wide.while_body.sunk | while | flops 2 | bytes 132205 | solution.py:74
  291.9 0.6 fusion.76
  292.5 2.0 bitcast_dynamic-update-slice_fusion.18
  294.5 0.6 fusion.76
  295.1 2.0 bitcast_dynamic-update-slice_fusion.18
  297.2 0.6 fusion.76
  297.7 2.0 bitcast_dynamic-update-slice_fusion.18
  299.8 0.6 fusion.76
  300.4 2.0 bitcast_dynamic-update-slice_fusion.18
  302.3 40.1 %custom-call.35 = f32[4,128,128]{1,2,0:T(8,128)S(1)} custom-call(f32[4,128,128]{2,1,0:T(8,128)} %get-tuple-element.9), custom_call_target="InvertDiagBlocksLowerTriangular" | custom-call | tf_op jit(solution)/shard_map/kernel_solve/triangular_solve | solution.py:74
  343.4 0.3 convolution_subtract_fusion.6
  345.0 0.3 convolution_subtract_fusion.3
  345.5 0.8 fusion.20
  (60 shorter events, 5.4 us)
Async XLA Ops:
  27.4 85.1 %all-to-all-start = ((bf16[16,32,4096]{2,1,0:T(8,128)(2,1)}), bf16[16,32,4096]{2,1,0:T(8,128)(2,1)}, u32[]{:S(2)}, u32[]{:S(2)}) async-start(bf16[16,32,4096]{2,1,0:T(8,128)(2,1)} %bitcast_dynamic-update-slice_fusion.1), calls=%async_computation | async-start | bytes 8388608 | tf_op jit(solution)/shard_map/gradient_exchange/all_to_all | solution.py:44
  120.8 3.3 collective-permute-start
  125.5 18.7 %collective-permute-start.1 = (f32[4,32,1024]{2,1,0:T(8,128)S(1)}, f32[4,32,1024]{2,1,0:T(8,128)S(1)}, u32[]{:S(2)}, u32[]{:S(2)}) collective-permute-start(f32[4,32,1024]{2,1,0:T(8,128)S(1)} %dynamic-slice_bitcast_fusion.1), channel_id=1, source_target_pairs={{0,2},{1,3},{2,0},{3,1},{4,6},{5,7},{6,4},{7,5},{8,10},{9,11},{10,... | collective-permute-start | bytes 1572872 | tf_op jit(solution)/shard_map/sketch_reduce/ppermute | solution.py:8
  144.3 17.7 %collective-permute-start.2 = (f32[2,32,1024]{2,1,0:T(8,128)S(1)}, f32[2,32,1024]{2,1,0:T(8,128)S(1)}, u32[]{:S(2)}, u32[]{:S(2)}) collective-permute-start(f32[2,32,1024]{2,1,0:T(8,128)S(1)} %dynamic-slice_bitcast_fusion.2), channel_id=1, source_target_pairs={{0,4},{1,5},{2,6},{3,7},{4,0},{5,1},{6,2},{7,3},{8,12},{9,13},{10,... | collective-permute-start | bytes 786440 | tf_op jit(solution)/shard_map/sketch_reduce/ppermute | solution.py:8
  162.0 8.4 %collective-permute-start.3 = (f32[1,32,1024]{2,1,0:T(8,128)S(1)}, f32[1,32,1024]{2,1,0:T(8,128)S(1)}, u32[]{:S(2)}, u32[]{:S(2)}) collective-permute-start(f32[1,32,1024]{2,1,0:T(8,128)S(1)} %constant_dynamic-slice_fusion.1), channel_id=1, source_target_pairs={{0,8},{1,9},{2,10},{3,11},{4,12},{5,13},{6,14},{7,15},{8,0},{9,1},... | collective-permute-start | bytes 393224 | tf_op jit(solution)/shard_map/sketch_reduce/ppermute | solution.py:8
  170.5 30.0 %copy-start = (f32[1,32,1024]{2,1,0:T(8,128)}, f32[1,32,1024]{2,1,0:T(8,128)S(1)}, u32[]{:S(2)}) copy-start(f32[1,32,1024]{2,1,0:T(8,128)S(1)} %dynamic-slice_add_fusion) | copy-start | bytes 393220
  170.5 8.2 %collective-permute-start.4 = (f32[1,32,1024]{2,1,0:T(8,128)S(1)}, f32[1,32,1024]{2,1,0:T(8,128)S(1)}, u32[]{:S(2)}, u32[]{:S(2)}) collective-permute-start(f32[1,32,1024]{2,1,0:T(8,128)S(1)} %dynamic-slice_add_fusion), channel_id=1, source_target_pairs={{0,8},{1,9},{2,10},{3,11},{4,12},{5,13},{6,14},{7,15},{8,0},{9,1},... | collective-permute-start | bytes 393224 | tf_op jit(solution)/shard_map/sketch_gather/ppermute | solution.py:8
  178.7 8.3 %collective-permute-start.5 = (f32[2,32,1024]{2,1,0:T(8,128)S(1)}, f32[2,32,1024]{2,1,0:T(8,128)S(1)}, u32[]{:S(2)}, u32[]{:S(2)}) collective-permute-start(f32[2,32,1024]{2,1,0:T(8,128)S(1)} %maximum_bitcast_fusion), channel_id=1, source_target_pairs={{0,4},{1,5},{2,6},{3,7},{4,0},{5,1},{6,2},{7,3},{8,12},{9,13},{10,... | collective-permute-start | bytes 786440 | tf_op jit(solution)/shard_map/sketch_gather/ppermute | solution.py:8
  178.8 21.8 %copy-start.2 = (s32[24]{0:T(128)S(1)}, s32[24]{0:T(128)}, u32[]{:S(2)}) copy-start(s32[24]{0:T(128)} %param.7) | copy-start | bytes 292
  178.8 21.9 %copy-start.1 = (s32[24,128]{1,0:T(8,128)S(1)}, s32[24,128]{1,0:T(8,128)}, u32[]{:S(2)}) copy-start(s32[24,128]{1,0:T(8,128)} %param.6) | copy-start | bytes 36868
  187.1 13.1 %collective-permute-start.6 = (f32[4,32,1024]{2,1,0:T(8,128)S(1)}, f32[4,32,1024]{2,1,0:T(8,128)S(1)}, u32[]{:S(2)}, u32[]{:S(2)}) collective-permute-start(f32[4,32,1024]{2,1,0:T(8,128)S(1)} %bitcast.148), channel_id=1, source_target_pairs={{0,2},{1,3},{2,0},{3,1},{4,6},{5,7},{6,4},{7,5},{8,10},{9,11},{10,... | collective-permute-start | bytes 1572872 | tf_op jit(solution)/shard_map/sketch_gather/ppermute | solution.py:8
  200.5 2.7 collective-permute-start.7
